TPU v7x, 512 devices: a whole 4x4x16 slice. The times are simulated.
512 devices in a mesh: grp: 16 (over z), lat: 32 (over y, x, core).
Axes of the slice: x: 4, y: 4, z: 16, core: 2. Of those that a mesh axis runs over, the one named last changes fastest.
Arguments:
- stream: bfloat16 [256, 8192], P('lat'), may hold values from -26 to 26
- batch_index: int32 [256], replicated, may hold values from 0 to 255
- weight: bfloat16 [8192, 65536], P(None, ('grp', 'lat')), may hold values from -0.26516504 to 0.26516504
- enc_bias: float32 [65536], P(('grp', 'lat')), may hold values from -1.5 to 0.5
- dec_bias: float32 [8192], replicated, may hold values from -3 to 3
Outputs:
- weight_grad: bfloat16 [8192, 65536], P(None, ('grp', 'lat'))
- bias_grad: float32 [65536], P(('grp', 'lat'))
- recon_error: bfloat16 [256, 8192], P('lat')
All inputs are finite; a program needn't handle non-finite values.
Results may differ from a plain program's by a relative error of at most 0.025.
Values may be sent and summed in bfloat16 or wider, within the bound.
No kernel may reach another device: no remote copies, remote signals or barrier semaphores. Data moves between devices by JAX's collectives and lax.ppermute only.
A program may use at most 64 MiB of HBM per device.

v0:
```python
import jax
import jax.numpy as jnp
import numpy as np
from jax import lax
from jax.sharding import Mesh
from jax.sharding import PartitionSpec as P

sharpness = 8.0
penalty = 0.25
epsilon = 1e-06
LAT = ("chip", "core")
ALL = ("grp", "chip", "core")


def xor_pairs(n, bit):
    return [(i, i ^ 1 << bit) for i in range(n)]


def butterfly_sum(x, axis, n, send_dtype):
    acc = x
    for bit in range(n.bit_length() - 1):
        sent = acc.astype(send_dtype)
        acc = sent.astype(jnp.float32) + lax.ppermute(sent, axis, xor_pairs(n, bit)).astype(
            jnp.float32
        )
    return acc


def swap_cores(x):
    return lax.ppermute(x, "core", [(0, 1), (1, 0)])


def body(stream, batch_index, weight, enc_bias, dec_bias):
    own_rows = stream.shape[0]
    n_chip = lax.axis_size("chip")
    n_grp = lax.axis_size("grp")
    chip = lax.axis_index("chip")
    core = lax.axis_index("core")
    half = n_chip * own_rows
    n_tok = batch_index.shape[0]
    mine = lax.all_gather(stream, "chip", axis=0, tiled=True)
    gathered = jnp.concatenate([mine, swap_cores(mine)], axis=0)
    q = jnp.arange(n_tok, dtype=jnp.int32)
    side = q // half
    q_chip = q % half // own_rows
    q_row = q % own_rows
    q_core = jnp.where(side == 0, core, 1 - core)
    token = (q_chip * 2 + q_core) * own_rows + q_row
    src = jnp.take(batch_index, token)
    s_chip = src // (2 * own_rows)
    s_core = src // own_rows % 2
    place = jnp.where(s_core == core, 0, half) + s_chip * own_rows + src % own_rows
    onehot = (
        place[:, None] == lax.broadcasted_iota(jnp.int32, (n_tok, gathered.shape[0]), 1)
    ).astype(gathered.dtype)
    batch = jnp.dot(onehot, gathered, preferred_element_type=jnp.float32).astype(jnp.bfloat16)
    centered = (batch.astype(jnp.float32) - dec_bias).astype(jnp.bfloat16)
    preact = jnp.dot(centered, weight, preferred_element_type=jnp.float32) + enc_bias
    active = (jax.nn.softplus(sharpness * preact) / sharpness).astype(jnp.bfloat16)
    own_batch = lax.dynamic_slice_in_dim(batch, chip * own_rows, own_rows, 0)
    partial = lax.dot_general(
        active, weight, (((1,), (1,)), ((), ())), preferred_element_type=jnp.float32
    ).astype(jnp.bfloat16)
    halves = partial.reshape(2, n_chip, own_rows, partial.shape[1])
    by_core = jnp.where(core == 0, halves, halves[::-1])
    lat_order = jnp.swapaxes(by_core, 0, 1).reshape(partial.shape)
    block_recon = lax.psum_scatter(lat_order, LAT, scatter_dimension=0, tiled=True)
    recon = butterfly_sum(block_recon.astype(jnp.float32), "grp", n_grp, jnp.bfloat16)
    error_own = recon + dec_bias - own_batch.astype(jnp.float32)
    grad_own = (2.0 * error_own).astype(jnp.bfloat16)
    grad_mine = lax.all_gather(grad_own, "chip", axis=0, tiled=True)
    grad_rows = jnp.concatenate([grad_mine, swap_cores(grad_mine)], axis=0)
    grad_active = jnp.dot(grad_rows, weight, preferred_element_type=jnp.float32)
    decoder_grad = lax.dot_general(
        grad_rows, active, (((0,), (0,)), ((), ())), preferred_element_type=jnp.float32
    )
    grad_pre = (grad_active + penalty) * jax.nn.sigmoid(sharpness * preact)
    encoder_grad = lax.dot_general(
        centered,
        grad_pre.astype(jnp.bfloat16),
        (((0,), (0,)), ((), ())),
        preferred_element_type=jnp.float32,
    )
    grad_raw = encoder_grad + decoder_grad
    bias_raw = jnp.sum(grad_pre, axis=0)
    local_squares = jnp.sum(grad_raw * grad_raw) + jnp.sum(bias_raw * bias_raw)
    squares = jnp.broadcast_to(local_squares, (1, 128))
    squares = butterfly_sum(squares, "core", 2, jnp.float32)
    squares = butterfly_sum(squares, "chip", n_chip, jnp.float32)
    total_squares = butterfly_sum(squares, "grp", n_grp, jnp.float32)[0, 0]
    entries = (weight.shape[0] + 1) * weight.shape[1] * 2 * n_chip * n_grp
    factor = jnp.minimum(1.0, 1.0 / jnp.sqrt(total_squares / entries + epsilon))
    return (
        (grad_raw * factor).astype(jnp.bfloat16),
        bias_raw * factor,
        error_own.astype(jnp.bfloat16),
    )


def solution(mesh):
    devices = np.asarray(mesh.devices)
    n_grp, n_lat = devices.shape
    split = Mesh(devices.reshape(n_grp, n_lat // 2, 2), ALL)
    return jax.shard_map(
        body,
        mesh=split,
        in_specs=(P(LAT, None), P(), P(None, ALL), P(ALL), P()),
        out_specs=(P(None, ALL), P(ALL), P(LAT, None)),
        check_vma=False,
    )
```

profile of v0, /device:TPU:2, one launch (start us, length us, event | category | flops | bytes accessed | tf_op | source)
XLA Modules:
  0.0 399.3 jit_solution(17982487750044333137)
XLA Ops:
  7.2 0.0 copy-start
  7.2 0.0 all-gather.3.cloned.1.call-start
  7.2 0.7 all-gather.3.cloned.1.call-update
  7.9 0.0 reduce-scatter.2.cloned.1.call-start
  8.0 67.5 %all-gather.3.cloned.1.call-done = bf16[128,8192]{1,0:T(8,128)(2,1)} async-done(((bf16[8,8192]{1,0:T(8,128)(2,1)}), bf16[128,8192]{1,0:T(8,128)(2,1)}) %all-gather.3.cloned.1.call-update) | async-done | bytes 2097168 | tf_op jit(solution)/shard_map/all_gather | solution.py:41
  75.4 1.9 collective-permute-start
  77.4 2.0 gather_fusion
  79.4 0.0 copy-start.3
  79.4 0.0 copy-start.4
  79.4 2.4 collective-permute-done
  81.8 3.5 convolution_convert_fusion.1
  85.3 0.0 copy-start.1
  85.4 1.9 copy-done.1
  87.3 0.0 copy-done
  87.3 0.0 copy-done.3
  87.3 0.0 copy-done.4
  87.3 1.3 fusion.7
  88.6 1.3 convolution_convert_fusion
  89.9 0.4 copy.11
  90.3 3.0 reverse_select_fusion
  93.4 0.0 reduce-scatter.2.cloned.1.call-update
  93.4 0.0 all-gather.5.cloned.1.call-start
  93.4 104.6 %reduce-scatter.2.cloned.1.call-done = bf16[8,8192]{1,0:T(8,128)(2,1)} async-done(((bf16[256,8192]{1,0:T(8,128)(2,1)}), bf16[8,8192]{1,0:T(8,128)(2,1)}) %reduce-scatter.2.cloned.1.call-update) | async-done | bytes 131088 | tf_op jit(solution)/shard_map/reduce_scatter | solution.py:67
  198.0 3.5 collective-permute-start.1
  201.5 3.6 collective-permute-done.1
  205.1 0.9 add_convert_fusion.2
  206.1 4.4 %collective-permute-start.2 = (bf16[8,8192]{1,0:T(8,128)(2,1)S(1)}, bf16[8,8192]{1,0:T(8,128)(2,1)S(1)}, u32[]{:S(2)}, u32[]{:S(2)}) collective-permute-start(bf16[8,8192]{1,0:T(8,128)(2,1)S(1)} %add_convert_fusion.2), channel_id=1, source_target_pairs={{0,64},{32,96},{64,0},{96,32},{128,192},{160,224},{192,128},{224,1... | collective-permute-start | bytes 393224 | tf_op jit(solution)/shard_map/ppermute | solution.py:23
  210.5 4.7 %collective-permute-done.2 = bf16[8,8192]{1,0:T(8,128)(2,1)S(1)} collective-permute-done((bf16[8,8192]{1,0:T(8,128)(2,1)S(1)}, bf16[8,8192]{1,0:T(8,128)(2,1)S(1)}, u32[]{:S(2)}, u32[]{:S(2)}) %collective-permute-start.2) | collective-permute-done | bytes 131104 | tf_op jit(solution)/shard_map/ppermute | solution.py:23
  215.3 8.0 %collective-permute-start.3 = (bf16[8,8192]{1,0:T(8,128)(2,1)S(1)}, bf16[8,8192]{1,0:T(8,128)(2,1)S(1)}, u32[]{:S(2)}, u32[]{:S(2)}) collective-permute-start(bf16[8,8192]{1,0:T(8,128)(2,1)S(1)} %add_convert_fusion.1), channel_id=1, source_target_pairs={{0,128},{32,160},{64,192},{96,224},{128,0},{160,32},{192,64},{224,... | collective-permute-start | bytes 393224 | tf_op jit(solution)/shard_map/ppermute | solution.py:23
  223.3 7.2 %collective-permute-done.3 = bf16[8,8192]{1,0:T(8,128)(2,1)S(1)} collective-permute-done((bf16[8,8192]{1,0:T(8,128)(2,1)S(1)}, bf16[8,8192]{1,0:T(8,128)(2,1)S(1)}, u32[]{:S(2)}, u32[]{:S(2)}) %collective-permute-start.3) | collective-permute-done | bytes 131104 | tf_op jit(solution)/shard_map/ppermute | solution.py:23
  230.5 11.7 %collective-permute-start.4 = (bf16[8,8192]{1,0:T(8,128)(2,1)S(1)}, bf16[8,8192]{1,0:T(8,128)(2,1)S(1)}, u32[]{:S(2)}, u32[]{:S(2)}) collective-permute-start(bf16[8,8192]{1,0:T(8,128)(2,1)S(1)} %add_convert_fusion), channel_id=1, source_target_pairs={{0,256},{32,288},{64,320},{96,352},{128,384},{160,416},{192,448},{... | collective-permute-start | bytes 393224 | tf_op jit(solution)/shard_map/ppermute | solution.py:23
  242.2 6.7 %collective-permute-done.4 = bf16[8,8192]{1,0:T(8,128)(2,1)S(1)} collective-permute-done((bf16[8,8192]{1,0:T(8,128)(2,1)S(1)}, bf16[8,8192]{1,0:T(8,128)(2,1)S(1)}, u32[]{:S(2)}, u32[]{:S(2)}) %collective-permute-start.4) | collective-permute-done | bytes 131104 | tf_op jit(solution)/shard_map/ppermute | solution.py:23
  249.0 1.7 fusion.8
  250.6 0.0 all-gather.5.cloned.1.call-update
  250.7 58.8 %all-gather.5.cloned.1.call-done = bf16[128,8192]{1,0:T(8,128)(2,1)} async-done(((bf16[8,8192]{1,0:T(8,128)(2,1)}), bf16[128,8192]{1,0:T(8,128)(2,1)}) %all-gather.5.cloned.1.call-update) | async-done | bytes 2097168 | tf_op jit(solution)/shard_map/all_gather | solution.py:71
  309.5 1.9 collective-permute-start.5
  311.4 1.7 constant_dynamic-update-slice_fusion.1
  313.1 2.6 collective-permute-done.5
  315.7 0.2 constant_dynamic-update-slice_fusion
  315.9 1.3 fusion.23
  317.2 0.6 multiply_reduce_fusion.1
  317.8 0.3 copy-done.2
  318.1 1.5 fusion.3
  319.6 4.4 %multiply_reduce_fusion = (f32[]{:T(128)}, f32[8192,128]{1,0:T(8,128)}) fusion(f32[8192,128]{1,0:T(8,128)S(1)} %fusion.3, bf16[256,8192]{1,0:T(8,128)(2,1)S(1)} %constant_dynamic-update-slice_fusion, f32[256,128]{1,0:T(8,128)S(1)} %fusion.7), kind=kOutput, calls=%fused_computation.10 | convolution fusion | flops 540278784 | bytes 12713988 | tf_op jit(solution)/shard_map/dot_general | solution.py:74
  325.3 2.0 collective-permute-start.6
  327.4 1.0 collective-permute-done.6
  328.3 2.8 collective-permute-start.7
  331.1 2.7 collective-permute-done.7
  333.7 4.0 collective-permute-start.8
  337.7 2.9 collective-permute-done.8
  340.7 2.2 collective-permute-start.9
  342.8 3.3 collective-permute-done.9
  346.1 3.4 collective-permute-start.10
  349.5 3.6 collective-permute-done.10
  353.0 3.5 collective-permute-start.11
  356.5 2.0 collective-permute-done.11
  358.5 4.4 %collective-permute-start.12 = (f32[1,128]{1,0:T(1,128)S(1)}, f32[1,128]{1,0:T(1,128)S(1)}, u32[]{:S(2)}, u32[]{:S(2)}) collective-permute-start(f32[1,128]{1,0:T(1,128)S(1)} %add.281), channel_id=1, source_target_pairs={{0,64},{32,96},{64,0},{96,32},{128,192},{160,224},{192,128},{224,1... | collective-permute-start | bytes 1544 | tf_op jit(solution)/shard_map/ppermute | solution.py:23
  362.9 1.9 collective-permute-done.12
  364.8 7.6 %collective-permute-start.13 = (f32[1,128]{1,0:T(1,128)S(1)}, f32[1,128]{1,0:T(1,128)S(1)}, u32[]{:S(2)}, u32[]{:S(2)}) collective-permute-start(f32[1,128]{1,0:T(1,128)S(1)} %add.282), channel_id=1, source_target_pairs={{0,128},{32,160},{64,192},{96,224},{128,0},{160,32},{192,64},{224,... | collective-permute-start | bytes 1544 | tf_op jit(solution)/shard_map/ppermute | solution.py:23
  372.4 1.7 collective-permute-done.13
  374.1 12.8 %collective-permute-start.14 = (f32[1,128]{1,0:T(1,128)S(1)}, f32[1,128]{1,0:T(1,128)S(1)}, u32[]{:S(2)}, u32[]{:S(2)}) collective-permute-start(f32[1,128]{1,0:T(1,128)S(1)} %add.283), channel_id=1, source_target_pairs={{0,256},{32,288},{64,320},{96,352},{128,384},{160,416},{192,448},{... | collective-permute-start | bytes 1544 | tf_op jit(solution)/shard_map/ppermute | solution.py:23
  386.9 1.5 collective-permute-done.14
  388.5 0.5 broadcast_multiply_fusion
  389.0 3.7 multiply_convert_fusion
  (16 shorter events, 0.2 us)
Async XLA Ops:
  7.2 80.1 %copy-start = (bf16[8192,128]{1,0:T(8,128)(2,1)S(1)}, bf16[8192,128]{1,0:T(8,128)(2,1)}, u32[]{:S(2)}) copy-start(bf16[8192,128]{1,0:T(8,128)(2,1)} %param.7) | copy-start | bytes 6291460
  7.2 68.3 %all-gather.3.cloned.1.call-start = ((), (), s32[]{:S(2)}) async-start(), calls=%async_computation.1 | async-start | bytes 2228224 | tf_op jit(solution)/shard_map/all_gather | solution.py:41
  7.9 190.1 %reduce-scatter.2.cloned.1.call-start = ((), (), s32[]{:S(2)}) async-start(), calls=%async_computation.2 | async-start | bytes 4325376 | tf_op jit(solution)/shard_map/reduce_scatter | solution.py:67
  75.4 6.4 %collective-permute-start = (bf16[128,8192]{1,0:T(8,128)(2,1)}, bf16[128,8192]{1,0:T(8,128)(2,1)}, u32[]{:S(2)}, u32[]{:S(2)}) collective-permute-start(bf16[128,8192]{1,0:T(8,128)(2,1)} %all-gather.3.cloned.1.call-done), channel_id=1, source_target_pairs={{0,1},{1,0},{2,3},{3,2},{4,5},{5,4},{6,7},{7,6},{8,9},{9,8},{10,11... | collective-permute-start | bytes 6291464 | tf_op jit(solution)/shard_map/ppermute | solution.py:30
  79.4 7.9 %copy-start.3 = (f32[8192]{0:T(1024)S(1)}, f32[8192]{0:T(1024)}, u32[]{:S(2)}) copy-start(f32[8192]{0:T(1024)} %param.9) | copy-start | bytes 98308
  79.4 7.9 %copy-start.4 = (f32[128]{0:T(128)S(1)}, f32[128]{0:T(128)}, u32[]{:S(2)}) copy-start(f32[128]{0:T(128)} %param.8) | copy-start | bytes 1540
  85.3 1.9 copy-start.1
  93.4 216.1 %all-gather.5.cloned.1.call-start = ((), (), s32[]{:S(2)}) async-start(), calls=%async_computation.3 | async-start | bytes 2228224 | tf_op jit(solution)/shard_map/all_gather | solution.py:71
  198.0 7.1 %collective-permute-start.1 = (bf16[8,8192]{1,0:T(8,128)(2,1)}, bf16[8,8192]{1,0:T(8,128)(2,1)S(1)}, u32[]{:S(2)}, u32[]{:S(2)}) collective-permute-start(bf16[8,8192]{1,0:T(8,128)(2,1)} %reduce-scatter.2.cloned.1.call-done), channel_id=1, source_target_pairs={{0,32},{32,0},{64,96},{96,64},{128,160},{160,128},{192,224},{224,1... | collective-permute-start | bytes 393224 | tf_op jit(solution)/shard_map/ppermute | solution.py:23
  206.1 9.2 %collective-permute-start.2 = (bf16[8,8192]{1,0:T(8,128)(2,1)S(1)}, bf16[8,8192]{1,0:T(8,128)(2,1)S(1)}, u32[]{:S(2)}, u32[]{:S(2)}) collective-permute-start(bf16[8,8192]{1,0:T(8,128)(2,1)S(1)} %add_convert_fusion.2), channel_id=1, source_target_pairs={{0,64},{32,96},{64,0},{96,32},{128,192},{160,224},{192,128},{224,1... | collective-permute-start | bytes 393224 | tf_op jit(solution)/shard_map/ppermute | solution.py:23
  215.3 15.2 %collective-permute-start.3 = (bf16[8,8192]{1,0:T(8,128)(2,1)S(1)}, bf16[8,8192]{1,0:T(8,128)(2,1)S(1)}, u32[]{:S(2)}, u32[]{:S(2)}) collective-permute-start(bf16[8,8192]{1,0:T(8,128)(2,1)S(1)} %add_convert_fusion.1), channel_id=1, source_target_pairs={{0,128},{32,160},{64,192},{96,224},{128,0},{160,32},{192,64},{224,... | collective-permute-start | bytes 393224 | tf_op jit(solution)/shard_map/ppermute | solution.py:23
  230.5 18.4 %collective-permute-start.4 = (bf16[8,8192]{1,0:T(8,128)(2,1)S(1)}, bf16[8,8192]{1,0:T(8,128)(2,1)S(1)}, u32[]{:S(2)}, u32[]{:S(2)}) collective-permute-start(bf16[8,8192]{1,0:T(8,128)(2,1)S(1)} %add_convert_fusion), channel_id=1, source_target_pairs={{0,256},{32,288},{64,320},{96,352},{128,384},{160,416},{192,448},{... | collective-permute-start | bytes 393224 | tf_op jit(solution)/shard_map/ppermute | solution.py:23
  309.5 6.3 %collective-permute-start.5 = (bf16[128,8192]{1,0:T(8,128)(2,1)}, bf16[128,8192]{1,0:T(8,128)(2,1)S(1)}, u32[]{:S(2)}, u32[]{:S(2)}) collective-permute-start(bf16[128,8192]{1,0:T(8,128)(2,1)} %all-gather.5.cloned.1.call-done), channel_id=1, source_target_pairs={{0,1},{1,0},{2,3},{3,2},{4,5},{5,4},{6,7},{7,6},{8,9},{9,8},{10,11... | collective-permute-start | bytes 6291464 | tf_op jit(solution)/shard_map/ppermute | solution.py:30
  315.9 2.2 copy-start.2
  325.3 3.0 collective-permute-start.6
  328.3 5.4 %collective-permute-start.7 = (f32[1,128]{1,0:T(1,128)S(1)}, f32[1,128]{1,0:T(1,128)S(1)}, u32[]{:S(2)}, u32[]{:S(2)}) collective-permute-start(f32[1,128]{1,0:T(1,128)S(1)} %broadcast_add_fusion), channel_id=1, source_target_pairs={{0,2},{2,0},{4,6},{6,4},{8,10},{10,8},{12,14},{14,12},{16,18},{18,... | collective-permute-start | bytes 1544 | tf_op jit(solution)/shard_map/ppermute | solution.py:23
  333.7 6.9 %collective-permute-start.8 = (f32[1,128]{1,0:T(1,128)S(1)}, f32[1,128]{1,0:T(1,128)S(1)}, u32[]{:S(2)}, u32[]{:S(2)}) collective-permute-start(f32[1,128]{1,0:T(1,128)S(1)} %fusion.30), channel_id=1, source_target_pairs={{0,4},{2,6},{4,0},{6,2},{8,12},{10,14},{12,8},{14,10},{16,20},{18,... | collective-permute-start | bytes 1544 | tf_op jit(solution)/shard_map/ppermute | solution.py:23
  340.7 5.4 %collective-permute-start.9 = (f32[1,128]{1,0:T(1,128)S(1)}, f32[1,128]{1,0:T(1,128)S(1)}, u32[]{:S(2)}, u32[]{:S(2)}) collective-permute-start(f32[1,128]{1,0:T(1,128)S(1)} %add.278), channel_id=1, source_target_pairs={{0,8},{2,10},{4,12},{6,14},{8,0},{10,2},{12,4},{14,6},{16,24},{18,... | collective-permute-start | bytes 1544 | tf_op jit(solution)/shard_map/ppermute | solution.py:23
  346.1 6.9 %collective-permute-start.10 = (f32[1,128]{1,0:T(1,128)S(1)}, f32[1,128]{1,0:T(1,128)S(1)}, u32[]{:S(2)}, u32[]{:S(2)}) collective-permute-start(f32[1,128]{1,0:T(1,128)S(1)} %add.279), channel_id=1, source_target_pairs={{0,16},{2,18},{4,20},{6,22},{8,24},{10,26},{12,28},{14,30},{16,0},... | collective-permute-start | bytes 1544 | tf_op jit(solution)/shard_map/ppermute | solution.py:23
  353.0 5.4 %collective-permute-start.11 = (f32[1,128]{1,0:T(1,128)S(1)}, f32[1,128]{1,0:T(1,128)S(1)}, u32[]{:S(2)}, u32[]{:S(2)}) collective-permute-start(f32[1,128]{1,0:T(1,128)S(1)} %add.280), channel_id=1, source_target_pairs={{0,32},{32,0},{64,96},{96,64},{128,160},{160,128},{192,224},{224,1... | collective-permute-start | bytes 1544 | tf_op jit(solution)/shard_map/ppermute | solution.py:23
  358.5 6.3 %collective-permute-start.12 = (f32[1,128]{1,0:T(1,128)S(1)}, f32[1,128]{1,0:T(1,128)S(1)}, u32[]{:S(2)}, u32[]{:S(2)}) collective-permute-start(f32[1,128]{1,0:T(1,128)S(1)} %add.281), channel_id=1, source_target_pairs={{0,64},{32,96},{64,0},{96,32},{128,192},{160,224},{192,128},{224,1... | collective-permute-start | bytes 1544 | tf_op jit(solution)/shard_map/ppermute | solution.py:23
  364.8 9.3 %collective-permute-start.13 = (f32[1,128]{1,0:T(1,128)S(1)}, f32[1,128]{1,0:T(1,128)S(1)}, u32[]{:S(2)}, u32[]{:S(2)}) collective-permute-start(f32[1,128]{1,0:T(1,128)S(1)} %add.282), channel_id=1, source_target_pairs={{0,128},{32,160},{64,192},{96,224},{128,0},{160,32},{192,64},{224,... | collective-permute-start | bytes 1544 | tf_op jit(solution)/shard_map/ppermute | solution.py:23
  374.1 14.3 %collective-permute-start.14 = (f32[1,128]{1,0:T(1,128)S(1)}, f32[1,128]{1,0:T(1,128)S(1)}, u32[]{:S(2)}, u32[]{:S(2)}) collective-permute-start(f32[1,128]{1,0:T(1,128)S(1)} %add.283), channel_id=1, source_target_pairs={{0,256},{32,288},{64,320},{96,352},{128,384},{160,416},{192,448},{... | collective-permute-start | bytes 1544 | tf_op jit(solution)/shard_map/ppermute | solution.py:23
Sparse Core Ops, SparseCore 0:
  11.0 64.3 all-gather.2
  93.5 104.5 reduce-scatter.1
  250.8 58.6 all-gather.4
where the time goes:
time: 400 us; the launch traced here: 399 us
  waiting for transfers between devices  279 us (70%)
  starting transfers between devices  74.1 us (19%)
  between operations  15.4 us (4%)
  matrix products  13.3 us (3%)
  other arithmetic  10.7 us (3%)
  local copies, waits for them, and re-layouts  6.56 us (2%)
    reduce_scatter x1, waiting for transfers between devices, body(): lax.psum_scatter(lat_order, LAT, scatter_dimension=0, tiled=True)  105 us
    ppermute x13, starting transfers between devices, butterfly_sum(): lax.ppermute(sent, axis, xor_pairs(n, bit)).astype(jnp.float32)  70.2 us
    all_gather x1, waiting for transfers between devices, body(): mine = lax.all_gather(stream, 'chip', axis=0, tiled=True)  67.5 us
    all_gather x1, waiting for transfers between devices, body(): grad_mine = lax.all_gather(grad_own, 'chip', axis=0, tiled=True)  58.8 us
    ppermute x13, waiting for transfers between devices, butterfly_sum(): lax.ppermute(sent, axis, xor_pairs(n, bit)).astype(jnp.float32)  42.7 us
  transfers between devices with their start and end apart: 18, of which 18 were waited for; matrix products, arithmetic and copies ran while one was open for 1% of the time, Pallas kernels for 0%

commit v1 on v0

--- a/solution.py
+++ b/solution.py
@@ -68,7 +68,9 @@
     recon = butterfly_sum(block_recon.astype(jnp.float32), "grp", n_grp, jnp.bfloat16)
     error_own = recon + dec_bias - own_batch.astype(jnp.float32)
     grad_own = (2.0 * error_own).astype(jnp.bfloat16)
-    grad_mine = lax.all_gather(grad_own, "chip", axis=0, tiled=True)
+    grad_mine = jnp.concatenate(
+        lax.all_to_all(jnp.stack([grad_own] * lax.axis_size("chip")), "chip", 0, 0), axis=0
+    )
     grad_rows = jnp.concatenate([grad_mine, swap_cores(grad_mine)], axis=0)
     grad_active = jnp.dot(grad_rows, weight, preferred_element_type=jnp.float32)
     decoder_grad = lax.dot_general(

time: 400 us -> 377 us (0.943)
  waiting for transfers between devices: 279 us -> 238 us
  blocking collectives: 0 us -> 36.7 us
  starting transfers between devices: 74.1 us -> 58 us
    all_gather x1 -> x0, waiting for transfers between devices: 58.8 us -> none  [body(): grad_mine = lax.all_gather(grad_own, 'chip', axis=0, tiled=True)]
    all_to_all x0 -> x1, blocking collectives: none -> 36.7 us  [body(): lax.all_to_all(jnp.stack([grad_own] * lax.axis_size('chip')), 'chip', 0, 0)]
    ppermute x13, starting transfers between devices: 70.2 us -> 53.8 us  [butterfly_sum(): lax.ppermute(sent, axis, xor_pairs(n, bit)).astype(jnp.float32)]
    ppermute x13, waiting for transfers between devices: 42.7 us -> 58.9 us  [butterfly_sum(): lax.ppermute(sent, axis, xor_pairs(n, bit)).astype(jnp.float32)]
  transfers between devices with their start and end apart: 18 -> 17, of which waited for: 18 -> 17; matrix products, arithmetic and copies ran while one was open for 1% -> 1% of each run, Pallas kernels for 0% -> 0%
where the time goes in v1:
time: 377 us
  waiting for transfers between devices  238 us (63%)
  starting transfers between devices  58 us (15%)
  blocking collectives  36.7 us (10%)
  between operations  15.7 us (4%)
  matrix products  12.8 us (3%)
  other arithmetic  10.6 us (3%)
  local copies, waits for them, and re-layouts  4.59 us (1%)
    reduce_scatter x1, waiting for transfers between devices, body(): lax.psum_scatter(lat_order, LAT, scatter_dimension=0, tiled=True)  105 us
    all_gather x1, waiting for transfers between devices, body(): mine = lax.all_gather(stream, 'chip', axis=0, tiled=True)  67.5 us
    ppermute x13, waiting for transfers between devices, butterfly_sum(): lax.ppermute(sent, axis, xor_pairs(n, bit)).astype(jnp.float32)  58.9 us
    ppermute x13, starting transfers between devices, butterfly_sum(): lax.ppermute(sent, axis, xor_pairs(n, bit)).astype(jnp.float32)  53.8 us
    all_to_all x1, blocking collectives, body(): lax.all_to_all(jnp.stack([grad_own] * lax.axis_size('chip')), 'chip', 0, 0)  36.7 us
  transfers between devices with their start and end apart: 17, of which 17 were waited for; matrix products, arithmetic and copies ran while one was open for 1% of the time, Pallas kernels for 0%

profile of v1, /device:TPU:2, one launch (start us, length us, event | category | flops | bytes accessed | tf_op | source)
XLA Modules:
  0.0 376.6 jit_solution(11228584562278177150)
XLA Ops:
  7.2 0.0 copy-start
  7.2 0.0 all-gather.2.cloned.1.call-start
  7.2 0.7 all-gather.2.cloned.1.call-update
  7.9 0.0 reduce-scatter.2.cloned.1.call-start
  8.0 67.5 %all-gather.2.cloned.1.call-done = bf16[128,8192]{1,0:T(8,128)(2,1)} async-done(((bf16[8,8192]{1,0:T(8,128)(2,1)}), bf16[128,8192]{1,0:T(8,128)(2,1)}) %all-gather.2.cloned.1.call-update) | async-done | bytes 2097168 | tf_op jit(solution)/shard_map/all_gather | solution.py:41
  75.4 1.9 collective-permute-start
  77.4 2.0 gather_fusion
  79.4 0.0 copy-start.3
  79.4 0.0 copy-start.4
  79.4 2.4 collective-permute-done
  81.8 3.5 convolution_convert_fusion.1
  85.3 0.0 copy-start.1
  85.4 2.0 copy-done.1
  87.3 0.0 copy-done
  87.3 0.0 copy-done.3
  87.3 0.0 copy-done.4
  87.3 1.3 fusion.9
  88.6 1.3 convolution_convert_fusion
  89.9 0.4 copy.11
  90.3 3.0 reverse_select_fusion
  93.3 0.0 reduce-scatter.2.cloned.1.call-update
  93.4 104.7 %reduce-scatter.2.cloned.1.call-done = bf16[8,8192]{1,0:T(8,128)(2,1)} async-done(((bf16[256,8192]{1,0:T(8,128)(2,1)}), bf16[8,8192]{1,0:T(8,128)(2,1)}) %reduce-scatter.2.cloned.1.call-update) | async-done | bytes 131088 | tf_op jit(solution)/shard_map/reduce_scatter | solution.py:67
  198.0 3.4 collective-permute-start.1
  201.5 3.6 collective-permute-done.1
  205.1 0.9 add_convert_fusion.2
  206.0 4.4 %collective-permute-start.2 = (bf16[8,8192]{1,0:T(8,128)(2,1)S(1)}, bf16[8,8192]{1,0:T(8,128)(2,1)S(1)}, u32[]{:S(2)}, u32[]{:S(2)}) collective-permute-start(bf16[8,8192]{1,0:T(8,128)(2,1)S(1)} %add_convert_fusion.2), channel_id=1, source_target_pairs={{0,64},{32,96},{64,0},{96,32},{128,192},{160,224},{192,128},{224,1... | collective-permute-start | bytes 393224 | tf_op jit(solution)/shard_map/ppermute | solution.py:23
  210.5 4.7 %collective-permute-done.2 = bf16[8,8192]{1,0:T(8,128)(2,1)S(1)} collective-permute-done((bf16[8,8192]{1,0:T(8,128)(2,1)S(1)}, bf16[8,8192]{1,0:T(8,128)(2,1)S(1)}, u32[]{:S(2)}, u32[]{:S(2)}) %collective-permute-start.2) | collective-permute-done | bytes 131104 | tf_op jit(solution)/shard_map/ppermute | solution.py:23
  215.2 8.0 %collective-permute-start.3 = (bf16[8,8192]{1,0:T(8,128)(2,1)S(1)}, bf16[8,8192]{1,0:T(8,128)(2,1)S(1)}, u32[]{:S(2)}, u32[]{:S(2)}) collective-permute-start(bf16[8,8192]{1,0:T(8,128)(2,1)S(1)} %add_convert_fusion.1), channel_id=1, source_target_pairs={{0,128},{32,160},{64,192},{96,224},{128,0},{160,32},{192,64},{224,... | collective-permute-start | bytes 393224 | tf_op jit(solution)/shard_map/ppermute | solution.py:23
  223.2 7.2 %collective-permute-done.3 = bf16[8,8192]{1,0:T(8,128)(2,1)S(1)} collective-permute-done((bf16[8,8192]{1,0:T(8,128)(2,1)S(1)}, bf16[8,8192]{1,0:T(8,128)(2,1)S(1)}, u32[]{:S(2)}, u32[]{:S(2)}) %collective-permute-start.3) | collective-permute-done | bytes 131104 | tf_op jit(solution)/shard_map/ppermute | solution.py:23
  230.5 11.7 %collective-permute-start.4 = (bf16[8,8192]{1,0:T(8,128)(2,1)S(1)}, bf16[8,8192]{1,0:T(8,128)(2,1)S(1)}, u32[]{:S(2)}, u32[]{:S(2)}) collective-permute-start(bf16[8,8192]{1,0:T(8,128)(2,1)S(1)} %add_convert_fusion), channel_id=1, source_target_pairs={{0,256},{32,288},{64,320},{96,352},{128,384},{160,416},{192,448},{... | collective-permute-start | bytes 393224 | tf_op jit(solution)/shard_map/ppermute | solution.py:23
  242.2 6.7 %collective-permute-done.4 = bf16[8,8192]{1,0:T(8,128)(2,1)S(1)} collective-permute-done((bf16[8,8192]{1,0:T(8,128)(2,1)S(1)}, bf16[8,8192]{1,0:T(8,128)(2,1)S(1)}, u32[]{:S(2)}, u32[]{:S(2)}) %collective-permute-start.4) | collective-permute-done | bytes 131104 | tf_op jit(solution)/shard_map/ppermute | solution.py:23
  248.9 1.6 fusion.10
  250.6 0.2 stack.2
  250.8 36.7 %all_to_all.5 = bf16[16,8,8192]{2,1,0:T(8,128)(2,1)S(1)} all-to-all(bf16[16,8,8192]{2,1,0:T(8,128)(2,1)S(1)} %stack.2), channel_id=1, replica_groups=mesh['grp'=16,'chip'=16,'core'=2] {'chip'}, dimensions={0} | all-to-all | bytes 4194304 | tf_op jit(solution)/shard_map/all_to_all | solution.py:72
  287.5 0.0 copy-start.2
  287.5 2.2 collective-permute-start.5
  289.7 4.1 %collective-permute-done.5 = bf16[128,8192]{1,0:T(8,128)(2,1)S(1)} collective-permute-done((bf16[128,8192]{1,0:T(8,128)(2,1)S(1)}, bf16[128,8192]{1,0:T(8,128)(2,1)S(1)}, u32[]{:S(2)}, u32[]{:S(2)}) %collective-permute-start.5) | collective-permute-done | bytes 2097184 | tf_op jit(solution)/shard_map/ppermute | solution.py:30
  293.8 1.3 fusion.27
  295.1 0.0 copy-done.2
  295.1 1.5 fusion.3
  296.6 0.6 multiply_reduce_fusion.1
  297.2 3.9 %multiply_reduce_fusion = (f32[]{:T(128)}, f32[8192,128]{1,0:T(8,128)}) fusion(f32[8192,128]{1,0:T(8,128)S(1)} %fusion.3, f32[256,128]{1,0:T(8,128)S(1)} %fusion.9, bf16[128,8192]{1,0:T(8,128)(2,1)S(1)} %collective-permute-done.5, bf16[128,8192]{1,0:T(8,128)(2,1)S(1)} %bitcast.16), kind=kOutput, calls=%fused_computation.11 | convolution fusion | flops 548667392 | bytes 12713988 | tf_op jit(solution)/shard_map/dot_general | solution.py:76
  302.4 2.0 collective-permute-start.6
  304.5 1.0 collective-permute-done.6
  305.4 3.4 collective-permute-start.7
  308.8 2.1 collective-permute-done.7
  310.9 2.7 collective-permute-start.8
  313.6 4.2 %collective-permute-done.8 = f32[1,128]{1,0:T(1,128)S(1)} collective-permute-done((f32[1,128]{1,0:T(1,128)S(1)}, f32[1,128]{1,0:T(1,128)S(1)}, u32[]{:S(2)}, u32[]{:S(2)}) %collective-permute-start.8) | collective-permute-done | bytes 544 | tf_op jit(solution)/shard_map/ppermute | solution.py:23
  317.8 1.9 collective-permute-start.9
  319.7 3.5 collective-permute-done.9
  323.2 2.7 collective-permute-start.10
  326.0 4.2 %collective-permute-done.10 = f32[1,128]{1,0:T(1,128)S(1)} collective-permute-done((f32[1,128]{1,0:T(1,128)S(1)}, f32[1,128]{1,0:T(1,128)S(1)}, u32[]{:S(2)}, u32[]{:S(2)}) %collective-permute-start.10) | collective-permute-done | bytes 544 | tf_op jit(solution)/shard_map/ppermute | solution.py:23
  330.2 1.9 collective-permute-start.11
  332.1 3.5 collective-permute-done.11
  335.6 1.9 collective-permute-start.12
  337.5 4.4 %collective-permute-done.12 = f32[1,128]{1,0:T(1,128)S(1)} collective-permute-done((f32[1,128]{1,0:T(1,128)S(1)}, f32[1,128]{1,0:T(1,128)S(1)}, u32[]{:S(2)}, u32[]{:S(2)}) %collective-permute-start.12) | collective-permute-done | bytes 544 | tf_op jit(solution)/shard_map/ppermute | solution.py:23
  341.9 1.9 collective-permute-start.13
  343.9 7.4 %collective-permute-done.13 = f32[1,128]{1,0:T(1,128)S(1)} collective-permute-done((f32[1,128]{1,0:T(1,128)S(1)}, f32[1,128]{1,0:T(1,128)S(1)}, u32[]{:S(2)}, u32[]{:S(2)}) %collective-permute-start.13) | collective-permute-done | bytes 544 | tf_op jit(solution)/shard_map/ppermute | solution.py:23
  351.3 7.8 %collective-permute-start.14 = (f32[1,128]{1,0:T(1,128)S(1)}, f32[1,128]{1,0:T(1,128)S(1)}, u32[]{:S(2)}, u32[]{:S(2)}) collective-permute-start(f32[1,128]{1,0:T(1,128)S(1)} %add.283), channel_id=1, source_target_pairs={{0,256},{32,288},{64,320},{96,352},{128,384},{160,416},{192,448},{... | collective-permute-start | bytes 1544 | tf_op jit(solution)/shard_map/ppermute | solution.py:23
  359.0 6.4 %collective-permute-done.14 = f32[1,128]{1,0:T(1,128)S(1)} collective-permute-done((f32[1,128]{1,0:T(1,128)S(1)}, f32[1,128]{1,0:T(1,128)S(1)}, u32[]{:S(2)}, u32[]{:S(2)}) %collective-permute-start.14) | collective-permute-done | bytes 544 | tf_op jit(solution)/shard_map/ppermute | solution.py:23
  365.5 0.5 broadcast_multiply_fusion
  366.0 3.7 multiply_convert_fusion
  (15 shorter events, 0.2 us)
Async XLA Ops:
  7.2 80.1 %copy-start = (bf16[8192,128]{1,0:T(8,128)(2,1)S(1)}, bf16[8192,128]{1,0:T(8,128)(2,1)}, u32[]{:S(2)}) copy-start(bf16[8192,128]{1,0:T(8,128)(2,1)} %param.7) | copy-start | bytes 6291460
  7.2 68.3 %all-gather.2.cloned.1.call-start = ((), (), s32[]{:S(2)}) async-start(), calls=%async_computation.2 | async-start | bytes 2228224 | tf_op jit(solution)/shard_map/all_gather | solution.py:41
  7.9 190.1 %reduce-scatter.2.cloned.1.call-start = ((), (), s32[]{:S(2)}) async-start(), calls=%async_computation.3 | async-start | bytes 4325376 | tf_op jit(solution)/shard_map/reduce_scatter | solution.py:67
  75.4 6.4 %collective-permute-start = (bf16[128,8192]{1,0:T(8,128)(2,1)}, bf16[128,8192]{1,0:T(8,128)(2,1)}, u32[]{:S(2)}, u32[]{:S(2)}) collective-permute-start(bf16[128,8192]{1,0:T(8,128)(2,1)} %all-gather.2.cloned.1.call-done), channel_id=1, source_target_pairs={{0,1},{1,0},{2,3},{3,2},{4,5},{5,4},{6,7},{7,6},{8,9},{9,8},{10,11... | collective-permute-start | bytes 6291464 | tf_op jit(solution)/shard_map/ppermute | solution.py:30
  79.4 7.9 %copy-start.3 = (f32[8192]{0:T(1024)S(1)}, f32[8192]{0:T(1024)}, u32[]{:S(2)}) copy-start(f32[8192]{0:T(1024)} %param.9) | copy-start | bytes 98308
  79.4 7.9 %copy-start.4 = (f32[128]{0:T(128)S(1)}, f32[128]{0:T(128)}, u32[]{:S(2)}) copy-start(f32[128]{0:T(128)} %param.8) | copy-start | bytes 1540
  85.3 2.0 copy-start.1
  198.0 7.1 %collective-permute-start.1 = (bf16[8,8192]{1,0:T(8,128)(2,1)}, bf16[8,8192]{1,0:T(8,128)(2,1)S(1)}, u32[]{:S(2)}, u32[]{:S(2)}) collective-permute-start(bf16[8,8192]{1,0:T(8,128)(2,1)} %reduce-scatter.2.cloned.1.call-done), channel_id=1, source_target_pairs={{0,32},{32,0},{64,96},{96,64},{128,160},{160,128},{192,224},{224,1... | collective-permute-start | bytes 393224 | tf_op jit(solution)/shard_map/ppermute | solution.py:23
  206.0 9.2 %collective-permute-start.2 = (bf16[8,8192]{1,0:T(8,128)(2,1)S(1)}, bf16[8,8192]{1,0:T(8,128)(2,1)S(1)}, u32[]{:S(2)}, u32[]{:S(2)}) collective-permute-start(bf16[8,8192]{1,0:T(8,128)(2,1)S(1)} %add_convert_fusion.2), channel_id=1, source_target_pairs={{0,64},{32,96},{64,0},{96,32},{128,192},{160,224},{192,128},{224,1... | collective-permute-start | bytes 393224 | tf_op jit(solution)/shard_map/ppermute | solution.py:23
  215.2 15.2 %collective-permute-start.3 = (bf16[8,8192]{1,0:T(8,128)(2,1)S(1)}, bf16[8,8192]{1,0:T(8,128)(2,1)S(1)}, u32[]{:S(2)}, u32[]{:S(2)}) collective-permute-start(bf16[8,8192]{1,0:T(8,128)(2,1)S(1)} %add_convert_fusion.1), channel_id=1, source_target_pairs={{0,128},{32,160},{64,192},{96,224},{128,0},{160,32},{192,64},{224,... | collective-permute-start | bytes 393224 | tf_op jit(solution)/shard_map/ppermute | solution.py:23
  230.5 18.4 %collective-permute-start.4 = (bf16[8,8192]{1,0:T(8,128)(2,1)S(1)}, bf16[8,8192]{1,0:T(8,128)(2,1)S(1)}, u32[]{:S(2)}, u32[]{:S(2)}) collective-permute-start(bf16[8,8192]{1,0:T(8,128)(2,1)S(1)} %add_convert_fusion), channel_id=1, source_target_pairs={{0,256},{32,288},{64,320},{96,352},{128,384},{160,416},{192,448},{... | collective-permute-start | bytes 393224 | tf_op jit(solution)/shard_map/ppermute | solution.py:23
  287.5 7.6 %copy-start.2 = (bf16[256,8192]{1,0:T(8,128)(2,1)S(1)}, bf16[256,8192]{1,0:T(8,128)(2,1)}, u32[]{:S(2)}) copy-start(bf16[256,8192]{1,0:T(8,128)(2,1)} %copy-done.1) | copy-start | bytes 12582916
  287.5 6.3 %collective-permute-start.5 = (bf16[128,8192]{1,0:T(8,128)(2,1)S(1)}, bf16[128,8192]{1,0:T(8,128)(2,1)S(1)}, u32[]{:S(2)}, u32[]{:S(2)}) collective-permute-start(bf16[128,8192]{1,0:T(8,128)(2,1)S(1)} %bitcast.14), channel_id=1, source_target_pairs={{0,1},{1,0},{2,3},{3,2},{4,5},{5,4},{6,7},{7,6},{8,9},{9,8},{10,11... | collective-permute-start | bytes 6291464 | tf_op jit(solution)/shard_map/ppermute | solution.py:30
  302.4 3.0 collective-permute-start.6
  305.4 5.4 %collective-permute-start.7 = (f32[1,128]{1,0:T(1,128)S(1)}, f32[1,128]{1,0:T(1,128)S(1)}, u32[]{:S(2)}, u32[]{:S(2)}) collective-permute-start(f32[1,128]{1,0:T(1,128)S(1)} %broadcast_add_fusion), channel_id=1, source_target_pairs={{0,2},{2,0},{4,6},{6,4},{8,10},{10,8},{12,14},{14,12},{16,18},{18,... | collective-permute-start | bytes 1544 | tf_op jit(solution)/shard_map/ppermute | solution.py:23
  310.9 6.9 %collective-permute-start.8 = (f32[1,128]{1,0:T(1,128)S(1)}, f32[1,128]{1,0:T(1,128)S(1)}, u32[]{:S(2)}, u32[]{:S(2)}) collective-permute-start(f32[1,128]{1,0:T(1,128)S(1)} %fusion.32), channel_id=1, source_target_pairs={{0,4},{2,6},{4,0},{6,2},{8,12},{10,14},{12,8},{14,10},{16,20},{18,... | collective-permute-start | bytes 1544 | tf_op jit(solution)/shard_map/ppermute | solution.py:23
  317.8 5.4 %collective-permute-start.9 = (f32[1,128]{1,0:T(1,128)S(1)}, f32[1,128]{1,0:T(1,128)S(1)}, u32[]{:S(2)}, u32[]{:S(2)}) collective-permute-start(f32[1,128]{1,0:T(1,128)S(1)} %add.278), channel_id=1, source_target_pairs={{0,8},{2,10},{4,12},{6,14},{8,0},{10,2},{12,4},{14,6},{16,24},{18,... | collective-permute-start | bytes 1544 | tf_op jit(solution)/shard_map/ppermute | solution.py:23
  323.2 6.9 %collective-permute-start.10 = (f32[1,128]{1,0:T(1,128)S(1)}, f32[1,128]{1,0:T(1,128)S(1)}, u32[]{:S(2)}, u32[]{:S(2)}) collective-permute-start(f32[1,128]{1,0:T(1,128)S(1)} %add.279), channel_id=1, source_target_pairs={{0,16},{2,18},{4,20},{6,22},{8,24},{10,26},{12,28},{14,30},{16,0},... | collective-permute-start | bytes 1544 | tf_op jit(solution)/shard_map/ppermute | solution.py:23
  330.2 5.4 %collective-permute-start.11 = (f32[1,128]{1,0:T(1,128)S(1)}, f32[1,128]{1,0:T(1,128)S(1)}, u32[]{:S(2)}, u32[]{:S(2)}) collective-permute-start(f32[1,128]{1,0:T(1,128)S(1)} %add.280), channel_id=1, source_target_pairs={{0,32},{32,0},{64,96},{96,64},{128,160},{160,128},{192,224},{224,1... | collective-permute-start | bytes 1544 | tf_op jit(solution)/shard_map/ppermute | solution.py:23
  335.6 6.3 %collective-permute-start.12 = (f32[1,128]{1,0:T(1,128)S(1)}, f32[1,128]{1,0:T(1,128)S(1)}, u32[]{:S(2)}, u32[]{:S(2)}) collective-permute-start(f32[1,128]{1,0:T(1,128)S(1)} %add.281), channel_id=1, source_target_pairs={{0,64},{32,96},{64,0},{96,32},{128,192},{160,224},{192,128},{224,1... | collective-permute-start | bytes 1544 | tf_op jit(solution)/shard_map/ppermute | solution.py:23
  341.9 9.3 %collective-permute-start.13 = (f32[1,128]{1,0:T(1,128)S(1)}, f32[1,128]{1,0:T(1,128)S(1)}, u32[]{:S(2)}, u32[]{:S(2)}) collective-permute-start(f32[1,128]{1,0:T(1,128)S(1)} %add.282), channel_id=1, source_target_pairs={{0,128},{32,160},{64,192},{96,224},{128,0},{160,32},{192,64},{224,... | collective-permute-start | bytes 1544 | tf_op jit(solution)/shard_map/ppermute | solution.py:23
  351.3 14.1 %collective-permute-start.14 = (f32[1,128]{1,0:T(1,128)S(1)}, f32[1,128]{1,0:T(1,128)S(1)}, u32[]{:S(2)}, u32[]{:S(2)}) collective-permute-start(f32[1,128]{1,0:T(1,128)S(1)} %add.283), channel_id=1, source_target_pairs={{0,256},{32,288},{64,320},{96,352},{128,384},{160,416},{192,448},{... | collective-permute-start | bytes 1544 | tf_op jit(solution)/shard_map/ppermute | solution.py:23
Sparse Core Ops, SparseCore 0:
  11.0 64.3 all-gather.1
  93.5 104.5 reduce-scatter.1
